TPU v7x, 512 devices: a whole 4x8x8 slice. The times are simulated.
512 devices in a mesh: req: 64 (over x, z, core), tp: 8 (over y).
Axes of the slice: x: 4, y: 8, z: 8, core: 2. Of those that a mesh axis runs over, the one named last changes fastest.
Arguments:
- residual_input: bfloat16 [8192, 3584], P('req', 'tp'), may hold values from -6 to 6
- new_token_queries: bfloat16 [8192, 4096], P('req', 'tp'), may hold values from -8 to 8
- new_token_keys: bfloat16 [8192, 2048], P('req', 'tp'), may hold values from -8 to 8
- new_token_values: bfloat16 [8192, 2048], P('req', 'tp'), may hold values from -6 to 6
- key_page_pool: bfloat16 [1536, 16, 2048], P('req', None, 'tp'), may hold values from -6 to 6
- value_page_pool: bfloat16 [1536, 16, 2048], P('req', None, 'tp'), may hold values from -6 to 6
- request_page_table: int32 [128, 64], P('req'), may hold values from -1 to 23, as said below
- page_token_length: int32 [128, 64], P('req'), may hold values from 0 to 16, as said below
- request_token_length: int32 [64, 2], P('req'), may hold values from 1 to 96, 128 in all within a row
- request_adapter: int32 [64, 2], P('req'), may hold values from 0 to 63
- adapter_table_row: int32 [64], replicated, may hold values from 0 to 63, each once
- output_weight: bfloat16 [4096, 3584], P('tp'), may hold values from -0.125 to 0.125
- adapter_down_weight: bfloat16 [64, 16, 4096], P('req', None, 'tp'), may hold values from -0.09375 to 0.09375
- adapter_up_weight: bfloat16 [64, 16, 3584], P('req', None, 'tp'), may hold values from -1.5 to 1.5
- norm_scale_row: float32 [3584], P('tp'), may hold values from 0.25 to 1.75
Outputs:
- hidden_out: bfloat16 [8192, 3584], P('req', 'tp')
Inputs may be any that keep to these rules, and one draw needn't show every extreme that they name: request_page_table[q, o] is a page of the pool of owner o (rows o * 24 to o * 24 + 23 of the pools), or -1; so the 2 requests of one index of req take at most 2 pages from one owner, and in every draw the requests of some index of req each take a page from every owner. Requests may share pages. `page_token_length`: 0 exactly where request_page_table is -1; every used page of a request is full but at most one.
All inputs are finite; a program needn't handle non-finite values.
Results may differ from a plain program's by a relative error of at most 0.015.
Values may be sent and summed in bfloat16 or wider, within the bound.
No kernel may reach another device: no remote copies, remote signals or barrier semaphores. Data moves between devices by JAX's collectives and lax.ppermute only.
A program may use at most 64 MiB of HBM per device.

v0:
```python
import jax
import jax.numpy as jnp
from jax import lax
from jax.sharding import PartitionSpec as P

HEAD_SIZE = 256


epsilon = 1e-06
adapter_scale = 2.0
masked_score = -1e30


def attend(
    query_rows, new_keys, new_values, gathered_keys, gathered_values, usable, prompt_lengths
):
    token_count = query_rows.shape[0]
    kv_heads = new_keys.shape[1] // HEAD_SIZE
    group_size = query_rows.shape[1] // new_keys.shape[1]
    requests_here = gathered_keys.shape[0]
    cached_count = gathered_keys.shape[1]
    query_heads = query_rows.reshape(token_count, kv_heads, group_size, HEAD_SIZE)
    past_keys = gathered_keys.reshape(requests_here, cached_count, kv_heads, HEAD_SIZE)
    past_values = gathered_values.reshape(requests_here * cached_count, kv_heads, HEAD_SIZE)
    fresh_keys = new_keys.reshape(token_count, kv_heads, HEAD_SIZE)
    fresh_values = new_values.reshape(token_count, kv_heads, HEAD_SIZE)
    positions = jnp.arange(token_count, dtype=jnp.int32)
    ends = jnp.cumsum(prompt_lengths)
    owner_request = jnp.sum((positions[:, None] >= ends[None, :]).astype(jnp.int32), axis=1)
    scaling = HEAD_SIZE ** (-0.5)
    past_scores = (
        jnp.einsum("tgqd,rngd->tgqrn", query_heads, past_keys, preferred_element_type=jnp.float32)
        * scaling
    )
    past_mask = usable[None, :, :] & (
        owner_request[:, None, None] == jnp.arange(requests_here, dtype=jnp.int32)[None, :, None]
    )
    past_scores = jnp.where(past_mask[:, None, None, :, :], past_scores, masked_score)
    past_scores = past_scores.reshape(
        token_count, kv_heads, group_size, requests_here * cached_count
    )
    fresh_scores = (
        jnp.einsum("tgqd,ugd->tgqu", query_heads, fresh_keys, preferred_element_type=jnp.float32)
        * scaling
    )
    fresh_mask = (owner_request[:, None] == owner_request[None, :]) & (
        positions[None, :] <= positions[:, None]
    )
    fresh_scores = jnp.where(fresh_mask[:, None, None, :], fresh_scores, masked_score)
    scores = jnp.concatenate([past_scores, fresh_scores], axis=3)
    highest = jnp.max(scores, axis=3, keepdims=True)
    weights = jnp.exp(scores - highest)
    weights = (weights / jnp.sum(weights, axis=3, keepdims=True)).astype(jnp.bfloat16)
    all_values = jnp.concatenate([past_values, fresh_values], axis=0)
    mixed = jnp.einsum("tgqk,kgd->tgqd", weights, all_values, preferred_element_type=jnp.float32)
    return mixed.reshape(token_count, -1).astype(jnp.bfloat16)


def local(
    residual_input,
    new_token_queries,
    new_token_keys,
    new_token_values,
    key_page_pool,
    value_page_pool,
    request_page_table,
    page_token_length,
    request_token_length,
    request_adapter,
    adapter_table_row,
    output_weight,
    adapter_down_weight,
    adapter_up_weight,
    norm_scale_row,
):
    owners = lax.axis_size("req")
    requests_here = request_page_table.shape[0]
    page_rows = key_page_pool.shape[1]
    token_count = new_token_queries.shape[0]
    width_part = residual_input.shape[1]
    wanted = lax.all_to_all(request_page_table, "req", split_axis=1, concat_axis=1, tiled=True)
    page_picks = jnp.maximum(wanted, 0)
    keys_out = key_page_pool[page_picks]
    values_out = value_page_pool[page_picks]
    keys_back, values_back = (
        lax.all_to_all(keys_out, "req", split_axis=1, concat_axis=1, tiled=True),
        lax.all_to_all(values_out, "req", split_axis=1, concat_axis=1, tiled=True),
    )
    gathered_keys = keys_back.reshape(requests_here, owners * page_rows, keys_back.shape[3])
    gathered_values = values_back.reshape(requests_here, owners * page_rows, values_back.shape[3])
    usable = (
        jnp.arange(page_rows, dtype=jnp.int32)[None, None, :] < page_token_length[:, :, None]
    ).reshape(requests_here, owners * page_rows)
    lengths = request_token_length[0]
    attention = attend(
        new_token_queries,
        new_token_keys,
        new_token_values,
        gathered_keys,
        gathered_values,
        usable,
        lengths,
    )
    adapters_all = adapter_table_row.shape[0]
    matches = request_adapter[0][:, None] == jnp.arange(adapters_all, dtype=jnp.int32)[None, :]
    chosen_pages = jnp.sum(jnp.where(matches, adapter_table_row[None, :], 0), axis=1)
    pieces = (
        lax.all_gather(adapter_down_weight, "req", axis=0, tiled=True),
        lax.all_gather(adapter_up_weight, "req", axis=0, tiled=True),
    )
    rows_here = pieces[0].shape[0]
    picker = (chosen_pages[:, None] == jnp.arange(rows_here, dtype=jnp.int32)[None, :]).astype(
        jnp.bfloat16
    )
    selected_input = jnp.einsum(
        "rk,kab->rab", picker, pieces[0], preferred_element_type=jnp.float32
    )
    selected_output = jnp.einsum(
        "rk,kab->rab", picker, pieces[1], preferred_element_type=jnp.float32
    )
    adapter_in = selected_input
    adapter_out = selected_output
    adapter_in = adapter_in.astype(jnp.bfloat16)
    adapter_out = adapter_out.astype(jnp.bfloat16)
    rank_size = adapter_in.shape[1]
    positions = jnp.arange(token_count, dtype=jnp.int32)
    ends = jnp.cumsum(lengths)
    owner_request = jnp.sum((positions[:, None] >= ends[None, :]).astype(jnp.int32), axis=1)
    selector = (
        owner_request[:, None] == jnp.arange(requests_here, dtype=jnp.int32)[None, :]
    ).astype(jnp.float32)
    selector_half = selector.astype(jnp.bfloat16)
    base_part = jnp.dot(attention, output_weight, preferred_element_type=jnp.float32)
    low_terms = jnp.einsum("tc,rkc->trk", attention, adapter_in, preferred_element_type=jnp.float32)
    low_part = jnp.sum(low_terms * selector[:, :, None], axis=1)
    base_output_full, low_sum = (
        lax.psum(base_part.astype(jnp.bfloat16), "tp").astype(jnp.float32),
        lax.psum(low_part.astype(jnp.bfloat16), "tp").astype(jnp.float32),
    )
    columns_full = lax.all_gather(adapter_out, "tp", axis=2, tiled=True)
    rows_masked = (low_sum.astype(jnp.bfloat16)[:, None, :] * selector_half[:, :, None]).reshape(
        token_count, requests_here * rank_size
    )
    projected_all_rows = base_output_full + adapter_scale * jnp.dot(
        rows_masked,
        columns_full.reshape(requests_here * rank_size, columns_full.shape[2]),
        preferred_element_type=jnp.float32,
    )
    mean_square = jnp.mean(projected_all_rows * projected_all_rows, axis=1)
    offset_cols = lax.axis_index("tp") * width_part
    projected_rows = lax.dynamic_slice_in_dim(projected_all_rows, offset_cols, width_part, 1)
    scaled = projected_rows * lax.rsqrt(mean_square + epsilon)[:, None]
    return (residual_input.astype(jnp.float32) + scaled * norm_scale_row).astype(jnp.bfloat16)


def solution(mesh):
    in_specs = (
        P("req", "tp"),
        P("req", "tp"),
        P("req", "tp"),
        P("req", "tp"),
        P("req", None, "tp"),
        P("req", None, "tp"),
        P("req", None),
        P("req", None),
        P("req", None),
        P("req", None),
        P(),
        P("tp", None),
        P("req", None, "tp"),
        P("req", None, "tp"),
        P("tp"),
    )
    out_specs = P("req", "tp")
    return jax.shard_map(local, mesh=mesh, in_specs=in_specs, out_specs=out_specs, check_vma=False)
```

profile of v0, /device:TPU:6, one launch (start us, length us, event | category | flops | bytes accessed | tf_op | source)
XLA Modules:
  0.0 221.0 jit_solution(12764904028897294609)
XLA Ops:
  7.4 0.8 copy.97
  8.2 21.4 %all_to_all.19 = s32[2,64,1]{0,2,1:T(1,128)S(1)} all-to-all(s32[2,64,1]{0,2,1:T(1,128)S(1)} %copy.97), channel_id=1, replica_groups=mesh['req'=64,'tp'=8] {'req'}, dimensions={1} | all-to-all | bytes 1024 | tf_op jit(solution)/shard_map/all_to_all | solution.py:81
  29.8 0.6 gather_fusion.1
  30.4 1.1 copy.103
  31.6 6.6 %all-to-all-start.2 = ((bf16[2,64,16,256]{3,2,0,1:T(8,128)(2,1)}), bf16[2,64,16,256]{3,2,0,1:T(8,128)(2,1)S(1)}, u32[]{:S(2)}, u32[]{:S(2)}) async-start(bf16[2,64,16,256]{3,2,0,1:T(8,128)(2,1)} %copy.103), calls=%async_computation.2 | async-start | bytes 2097152 | tf_op jit(solution)/shard_map/all_to_all | solution.py:86
  38.2 0.6 gather_fusion
  38.9 1.2 copy.99
  40.1 24.7 %all-to-all-done.2 = bf16[2,64,16,256]{3,2,0,1:T(8,128)(2,1)S(1)} async-done(((bf16[2,64,16,256]{3,2,0,1:T(8,128)(2,1)}), bf16[2,64,16,256]{3,2,0,1:T(8,128)(2,1)S(1)}, u32[]{:S(2)}, u32[]{:S(2)}) %all-to-all-start.2) | async-done | bytes 1048608 | tf_op jit(solution)/shard_map/all_to_all | solution.py:86
  64.8 8.1 %all-to-all-start.1 = ((bf16[2,64,16,256]{3,2,0,1:T(8,128)(2,1)}), bf16[2,64,16,256]{3,2,0,1:T(8,128)(2,1)S(1)}, u32[]{:S(2)}, u32[]{:S(2)}) async-start(bf16[2,64,16,256]{3,2,0,1:T(8,128)(2,1)} %copy.99), calls=%async_computation.1 | async-start | bytes 2097152 | tf_op jit(solution)/shard_map/all_to_all | solution.py:87
  72.9 0.7 all-gather.2.cloned.1.call-update
  74.1 0.2 reduce-window.8
  74.4 0.5 fusion.33
  74.9 0.2 fusion.28
  75.2 0.3 broadcast_and_fusion
  75.6 0.2 fusion.35
  75.9 0.5 fusion.34
  76.6 23.0 %all-to-all-done.1 = bf16[2,64,16,256]{3,2,0,1:T(8,128)(2,1)S(1)} async-done(((bf16[2,64,16,256]{3,2,0,1:T(8,128)(2,1)}), bf16[2,64,16,256]{3,2,0,1:T(8,128)(2,1)S(1)}, u32[]{:S(2)}, u32[]{:S(2)}) %all-to-all-start.1) | async-done | bytes 1048608 | tf_op jit(solution)/shard_map/all_to_all | solution.py:87
  99.5 1.1 copy.100
  100.6 1.5 copy.102
  102.2 0.3 fusion.5
  102.5 1.6 convolution_convert_fusion.1
  104.1 0.5 copy-done.2
  104.6 2.5 %convolution_convert_fusion = bf16[128,3584]{0,1:T(8,128)(2,1)} fusion(bf16[128,512]{0,1:T(8,128)(2,1)S(1)} %bitcast.80, bf16[512,3584]{1,0:T(8,128)(2,1)S(1)} %copy-done.2), kind=kOutput, calls=%fused_computation.5 | convolution fusion | flops 470220800 | bytes 4718592 | tf_op jit(solution)/shard_map/dot_general | solution.py:133
  107.1 49.5 %all_gather.10 = bf16[64,16,448]{2,1,0:T(8,128)(2,1)S(1)} all-gather(bf16[1,16,448]{2,1,0:T(8,128)(2,1)S(1)} %copy-done.6), channel_id=1, replica_groups=mesh['req'=64,'tp'=8] {'req'}, dimensions={0}, use_global_device_ids=true | all-gather | bytes 931840 | tf_op jit(solution)/shard_map/all_gather | solution.py:109
  156.6 1.2 convolution_convert_fusion.2
  157.8 0.2 copy.115
  158.0 34.0 %all_gather.11 = bf16[2,16,3584]{1,0,2:T(2,128)(2,1)S(1)} all-gather(bf16[2,16,448]{1,0,2:T(2,128)(2,1)S(1)} %copy.115), channel_id=1, replica_groups=mesh['req'=64,'tp'=8] {'tp'}, dimensions={2}, use_global_device_ids=true | all-gather | bytes 258048 | tf_op jit(solution)/shard_map/all_gather | solution.py:140
  192.0 2.4 %convolution_convert_fusion.3 = bf16[2,16,512]{2,0,1:T(2,128)(2,1)S(1)} fusion(bf16[64,16,512]{2,1,0:T(8,128)(2,1)} %all-gather.2.cloned.1.call-done, s32[2]{0:T(128)S(1)} %fusion.28), kind=kOutput, calls=%fused_computation.21 | convolution fusion | flops 2113664 | bytes 1081352 | tf_op jit(solution)/shard_map/rk,kab->rab/dot_general | solution.py:115
  194.4 0.1 fusion.13
  194.6 16.2 %psum.15 = bf16[128,16]{0,1:T(8,128)(2,1)S(1)} all-reduce(bf16[128,16]{0,1:T(8,128)(2,1)S(1)} %fusion.13), channel_id=1, replica_groups=mesh['req'=64,'tp'=8] {'tp'}, use_global_device_ids=true, to_apply=%region_8.9 | all-reduce | flops 2048 | bytes 8192 | tf_op jit(solution)/shard_map/psum | solution.py:138
  210.8 2.0 multiply_reduce_fusion
  212.8 0.8 add_convert_fusion
  (50 shorter events, 1.1 us)
Async XLA Ops:
  7.4 22.4 %copy-start = (bf16[24,16,256]{2,1,0:T(8,128)(2,1)S(1)}, bf16[24,16,256]{2,1,0:T(8,128)(2,1)}, u32[]{:S(2)}) copy-start(bf16[24,16,256]{2,1,0:T(8,128)(2,1)} %param.19) | copy-start | bytes 589828
  30.4 7.7 %copy-start.1 = (bf16[24,16,256]{2,1,0:T(8,128)(2,1)S(1)}, bf16[24,16,256]{2,1,0:T(8,128)(2,1)}, u32[]{:S(2)}) copy-start(bf16[24,16,256]{2,1,0:T(8,128)(2,1)} %param.20) | copy-start | bytes 589828
  31.6 33.2 %all-to-all-start.2 = ((bf16[2,64,16,256]{3,2,0,1:T(8,128)(2,1)}), bf16[2,64,16,256]{3,2,0,1:T(8,128)(2,1)S(1)}, u32[]{:S(2)}, u32[]{:S(2)}) async-start(bf16[2,64,16,256]{3,2,0,1:T(8,128)(2,1)} %copy.103), calls=%async_computation.2 | async-start | bytes 2097152 | tf_op jit(solution)/shard_map/all_to_all | solution.py:86
  38.8 34.9 %copy-start.8 = (s32[2,64]{1,0:T(2,128)S(1)}, s32[2,64]{1,0:T(2,128)}, u32[]{:S(2)}) copy-start(s32[2,64]{1,0:T(2,128)} %param.22) | copy-start | bytes 1540
  38.8 35.1 %copy-start.5 = (bf16[128,256]{1,0:T(8,128)(2,1)S(1)}, bf16[128,256]{1,0:T(8,128)(2,1)}, u32[]{:S(2)}) copy-start(bf16[128,256]{1,0:T(8,128)(2,1)} %param.18) | copy-start | bytes 196612
  38.9 35.2 %copy-start.12 = (s32[1,2]{1,0:T(1,128)S(1)}, s32[1,2]{1,0:T(1,128)}, u32[]{:S(2)}) copy-start(s32[1,2]{1,0:T(1,128)} %param.23) | copy-start | bytes 28
  38.9 36.0 %copy-start.13 = (s32[64]{0:T(128)S(1)}, s32[64]{0:T(128)}, u32[]{:S(2)}) copy-start(s32[64]{0:T(128)} %param.25) | copy-start | bytes 772
  38.9 36.0 %copy-start.14 = (s32[1,2]{1,0:T(1,128)S(1)}, s32[1,2]{1,0:T(1,128)}, u32[]{:S(2)}) copy-start(s32[1,2]{1,0:T(1,128)} %param.24) | copy-start | bytes 28
  40.1 35.5 %copy-start.10 = (bf16[128,512]{1,0:T(8,128)(2,1)S(1)}, bf16[128,512]{1,0:T(8,128)(2,1)}, u32[]{:S(2)}) copy-start(bf16[128,512]{1,0:T(8,128)(2,1)} %param.16) | copy-start | bytes 393220
  40.1 35.5 %copy-start.11 = (bf16[128,256]{1,0:T(8,128)(2,1)S(1)}, bf16[128,256]{1,0:T(8,128)(2,1)}, u32[]{:S(2)}) copy-start(bf16[128,256]{1,0:T(8,128)(2,1)} %param.17) | copy-start | bytes 196612
  64.8 34.7 %all-to-all-start.1 = ((bf16[2,64,16,256]{3,2,0,1:T(8,128)(2,1)}), bf16[2,64,16,256]{3,2,0,1:T(8,128)(2,1)S(1)}, u32[]{:S(2)}, u32[]{:S(2)}) async-start(bf16[2,64,16,256]{3,2,0,1:T(8,128)(2,1)} %copy.99), calls=%async_computation.1 | async-start | bytes 2097152 | tf_op jit(solution)/shard_map/all_to_all | solution.py:87
  72.9 119.1 %all-gather.2.cloned.1.call-start = ((), (), s32[]{:S(2)}) async-start(), calls=%async_computation.4 | async-start | bytes 1064960 | tf_op jit(solution)/shard_map/all_gather | solution.py:108
  73.6 137.2 %all-reduce.2.cloned.1.call-start = ((), (), s32[]{:S(2)}) async-start(), calls=%async_computation.3 | async-start | bytes 1835008 | tf_op jit(solution)/shard_map/psum | solution.py:137
  75.8 26.4 %copy-start.3 = (f32[128,1,2,128]{0,3,2,1:T(8,128)}, f32[128,1,2,128]{0,3,2,1:T(8,128)S(1)}, u32[]{:S(2)}) copy-start(f32[128,1,2,128]{0,3,2,1:T(8,128)S(1)} %get-tuple-element.11) | copy-start | bytes 393220
  102.5 2.1 copy-start.2
  104.6 2.6 %copy-start.6 = (bf16[1,16,448]{2,1,0:T(8,128)(2,1)S(1)}, bf16[1,16,448]{2,1,0:T(8,128)(2,1)}, u32[]{:S(2)}) copy-start(bf16[1,16,448]{2,1,0:T(8,128)(2,1)} %param.28) | copy-start | bytes 43012
  156.6 54.2 %copy-start.9 = (bf16[128,2]{0,1:T(2,128)(2,1)S(1)}, bf16[128,2]{0,1:T(2,128)(2,1)}, u32[]{:S(2)}) copy-start(bf16[128,2]{0,1:T(2,128)(2,1)} %get-tuple-element.6) | copy-start | bytes 1540
  210.8 2.0 copy-start.4
  210.8 2.0 copy-start.7
Sparse Core Ops, SparseCore 0:
  77.1 83.0 all-gather.1
Sparse Core Ops, SparseCore 1:
  107.2 81.3 all-reduce.1
where the time goes:
time: 222 us; the launch traced here: 221 us
  blocking collectives  121 us (55%)
  waiting for transfers between devices  48.4 us (22%)
  between operations  15.2 us (7%)
  starting transfers between devices  14.8 us (7%)
  matrix products  10.7 us (5%)
  local copies, waits for them, and re-layouts  8.48 us (4%)
  other arithmetic  2.52 us (1%)
    all_gather x1, blocking collectives, local(): lax.all_gather(adapter_up_weight, 'req', axis=0, tiled=True)  49.5 us
    all_gather x1, blocking collectives, local(): columns_full = lax.all_gather(adapter_out, 'tp', axis=2, tiled=True)  34 us
    all_to_all x1, waiting for transfers between devices, local(): lax.all_to_all(keys_out, 'req', split_axis=1, concat_axis=1, tiled=True)  24.7 us
    all_to_all x1, waiting for transfers between devices, local(): lax.all_to_all(values_out, 'req', split_axis=1, concat_axis=1, tiled=True)  23 us
    all_to_all x1, blocking collectives, local(): lax.all_to_all(request_page_table, 'req', split_axis=1, concat_axis=1, ti...  21.4 us
    psum x1, blocking collectives, local(): lax.psum(low_part.astype(jnp.bfloat16), 'tp').astype(jnp.float32)  16.2 us
    all_to_all x1, starting transfers between devices, local(): lax.all_to_all(values_out, 'req', split_axis=1, concat_axis=1, tiled=True)  8.09 us
    all_to_all x1, starting transfers between devices, local(): lax.all_to_all(keys_out, 'req', split_axis=1, concat_axis=1, tiled=True)  6.57 us
  transfers between devices with their start and end apart: 4, of which 2 were waited for; matrix products, arithmetic and copies ran while one was open for 7% of the time, Pallas kernels for 0%

commit v1 on v0

--- a/solution.py
+++ b/solution.py
@@ -12,7 +12,7 @@
 
 
 def attend(
-    query_rows, new_keys, new_values, gathered_keys, gathered_values, usable, prompt_lengths
+    query_rows, new_keys, new_values, gathered_keys, gathered_values, usable, owner_request
 ):
     token_count = query_rows.shape[0]
     kv_heads = new_keys.shape[1] // HEAD_SIZE
@@ -25,8 +25,6 @@
     fresh_keys = new_keys.reshape(token_count, kv_heads, HEAD_SIZE)
     fresh_values = new_values.reshape(token_count, kv_heads, HEAD_SIZE)
     positions = jnp.arange(token_count, dtype=jnp.int32)
-    ends = jnp.cumsum(prompt_lengths)
-    owner_request = jnp.sum((positions[:, None] >= ends[None, :]).astype(jnp.int32), axis=1)
     scaling = HEAD_SIZE ** (-0.5)
     past_scores = (
         jnp.einsum("tgqd,rngd->tgqrn", query_heads, past_keys, preferred_element_type=jnp.float32)
@@ -74,24 +72,32 @@
     norm_scale_row,
 ):
     owners = lax.axis_size("req")
+    groups = lax.axis_size("tp")
     requests_here = request_page_table.shape[0]
     page_rows = key_page_pool.shape[1]
     token_count = new_token_queries.shape[0]
     width_part = residual_input.shape[1]
+    head_cols = key_page_pool.shape[2]
+    down_cols = adapter_down_weight.shape[2]
+
+    adapter_pair = jnp.concatenate([adapter_down_weight, adapter_up_weight], axis=2)
+    adapters_everywhere = lax.all_gather(adapter_pair, "req", axis=0, tiled=True)
+
     wanted = lax.all_to_all(request_page_table, "req", split_axis=1, concat_axis=1, tiled=True)
     page_picks = jnp.maximum(wanted, 0)
-    keys_out = key_page_pool[page_picks]
-    values_out = value_page_pool[page_picks]
-    keys_back, values_back = (
-        lax.all_to_all(keys_out, "req", split_axis=1, concat_axis=1, tiled=True),
-        lax.all_to_all(values_out, "req", split_axis=1, concat_axis=1, tiled=True),
-    )
-    gathered_keys = keys_back.reshape(requests_here, owners * page_rows, keys_back.shape[3])
-    gathered_values = values_back.reshape(requests_here, owners * page_rows, values_back.shape[3])
+    kv_pool = jnp.concatenate([key_page_pool, value_page_pool], axis=2)
+    kv_out = kv_pool[page_picks]
+    kv_back = lax.all_to_all(kv_out, "req", split_axis=1, concat_axis=1, tiled=True)
+    kv_back = kv_back.reshape(requests_here, owners * page_rows, 2 * head_cols)
+    gathered_keys = kv_back[:, :, :head_cols]
+    gathered_values = kv_back[:, :, head_cols:]
     usable = (
         jnp.arange(page_rows, dtype=jnp.int32)[None, None, :] < page_token_length[:, :, None]
     ).reshape(requests_here, owners * page_rows)
     lengths = request_token_length[0]
+    positions = jnp.arange(token_count, dtype=jnp.int32)
+    ends = jnp.cumsum(lengths)
+    owner_request = jnp.sum((positions[:, None] >= ends[None, :]).astype(jnp.int32), axis=1)
     attention = attend(
         new_token_queries,
         new_token_keys,
@@ -99,33 +105,23 @@
         gathered_keys,
         gathered_values,
         usable,
-        lengths,
+        owner_request,
     )
+
     adapters_all = adapter_table_row.shape[0]
     matches = request_adapter[0][:, None] == jnp.arange(adapters_all, dtype=jnp.int32)[None, :]
     chosen_pages = jnp.sum(jnp.where(matches, adapter_table_row[None, :], 0), axis=1)
-    pieces = (
-        lax.all_gather(adapter_down_weight, "req", axis=0, tiled=True),
-        lax.all_gather(adapter_up_weight, "req", axis=0, tiled=True),
-    )
-    rows_here = pieces[0].shape[0]
+    rows_here = adapters_everywhere.shape[0]
     picker = (chosen_pages[:, None] == jnp.arange(rows_here, dtype=jnp.int32)[None, :]).astype(
         jnp.bfloat16
     )
-    selected_input = jnp.einsum(
-        "rk,kab->rab", picker, pieces[0], preferred_element_type=jnp.float32
-    )
-    selected_output = jnp.einsum(
-        "rk,kab->rab", picker, pieces[1], preferred_element_type=jnp.float32
-    )
-    adapter_in = selected_input
-    adapter_out = selected_output
-    adapter_in = adapter_in.astype(jnp.bfloat16)
-    adapter_out = adapter_out.astype(jnp.bfloat16)
+    selected = jnp.einsum(
+        "rk,kab->rab", picker, adapters_everywhere, preferred_element_type=jnp.float32
+    ).astype(jnp.bfloat16)
+    adapter_in = selected[:, :, :down_cols]
+    adapter_out = selected[:, :, down_cols:]
     rank_size = adapter_in.shape[1]
-    positions = jnp.arange(token_count, dtype=jnp.int32)
-    ends = jnp.cumsum(lengths)
-    owner_request = jnp.sum((positions[:, None] >= ends[None, :]).astype(jnp.int32), axis=1)
+
     selector = (
         owner_request[:, None] == jnp.arange(requests_here, dtype=jnp.int32)[None, :]
     ).astype(jnp.float32)
@@ -133,23 +129,33 @@
     base_part = jnp.dot(attention, output_weight, preferred_element_type=jnp.float32)
     low_terms = jnp.einsum("tc,rkc->trk", attention, adapter_in, preferred_element_type=jnp.float32)
     low_part = jnp.sum(low_terms * selector[:, :, None], axis=1)
-    base_output_full, low_sum = (
-        lax.psum(base_part.astype(jnp.bfloat16), "tp").astype(jnp.float32),
-        lax.psum(low_part.astype(jnp.bfloat16), "tp").astype(jnp.float32),
+
+    base_slots = base_part.astype(jnp.bfloat16).reshape(token_count, groups, width_part)
+    base_slots = jnp.transpose(base_slots, (1, 0, 2))
+    low_slots = jnp.broadcast_to(
+        low_part.astype(jnp.bfloat16)[None], (groups, token_count, rank_size)
     )
-    columns_full = lax.all_gather(adapter_out, "tp", axis=2, tiled=True)
+    pad_cols = (-(width_part + rank_size)) % 128
+    slots = jnp.concatenate(
+        [base_slots, low_slots, jnp.zeros((groups, token_count, pad_cols), jnp.bfloat16)], axis=2
+    )
+    arrived = lax.all_to_all(slots, "tp", split_axis=0, concat_axis=0, tiled=True)
+    arrived = arrived.astype(jnp.float32)
+    base_local = jnp.sum(arrived[:, :, :width_part], axis=0)
+    low_sum = jnp.sum(arrived[:, :, width_part:width_part + rank_size], axis=0)
+
     rows_masked = (low_sum.astype(jnp.bfloat16)[:, None, :] * selector_half[:, :, None]).reshape(
         token_count, requests_here * rank_size
     )
-    projected_all_rows = base_output_full + adapter_scale * jnp.dot(
+    projected = base_local + adapter_scale * jnp.dot(
         rows_masked,
-        columns_full.reshape(requests_here * rank_size, columns_full.shape[2]),
+        adapter_out.reshape(requests_here * rank_size, width_part),
         preferred_element_type=jnp.float32,
     )
-    mean_square = jnp.mean(projected_all_rows * projected_all_rows, axis=1)
-    offset_cols = lax.axis_index("tp") * width_part
-    projected_rows = lax.dynamic_slice_in_dim(projected_all_rows, offset_cols, width_part, 1)
-    scaled = projected_rows * lax.rsqrt(mean_square + epsilon)[:, None]
+    square_part = jnp.sum(projected * projected, axis=1)
+    square_sum = lax.psum(square_part, "tp")
+    mean_square = square_sum / (groups * width_part)
+    scaled = projected * lax.rsqrt(mean_square + epsilon)[:, None]
     return (residual_input.astype(jnp.float32) + scaled * norm_scale_row).astype(jnp.bfloat16)
 
 

time: 222 us -> 187 us (0.84)
  blocking collectives: 121 us -> 14.7 us
  waiting for transfers between devices: 48.4 us -> 104 us
  starting transfers between devices: 14.8 us -> 27.5 us
  local copies, waits for them, and re-layouts: 8.48 us -> 12.1 us
  other arithmetic: 2.52 us -> 5.9 us
  matrix products: 10.7 us -> 7.87 us
    all_gather x2 -> x0, blocking collectives: 83.4 us -> none  [the longest x1 49.5 us: local(): lax.all_gather(adapter_up_weight, 'req', axis=0, tiled=True)]
    all_gather x1, waiting for transfers between devices: 0.01 us -> 69.9 us  [local(): lax.all_gather(adapter_pair, 'req', axis=0, tiled=True)]
    all_to_all x1 -> x0, blocking collectives: 21.4 us -> none  [local(): lax.all_to_all(request_page_table, 'req', split_axis=1, concat_axis=1, ti...]
    all_to_all x2 -> x3, waiting for transfers between devices: 47.7 us -> 34.2 us  [the longest x1 29.2 us: local(): lax.all_to_all(slots, 'tp', split_axis=0, concat_axis=0, tiled=True)]
    all_to_all x2 -> x3, starting transfers between devices: 14.7 us -> 27.4 us  [the longest x1 14 us: local(): lax.all_to_all(request_page_table, 'req', split_axis=1, concat_axis=1, ti...]
    unnamed x31 -> x33, local copies, waits for them, and re-layouts: 0.64 us -> 5.44 us
    concatenate x0 -> x3, other arithmetic: none -> 3.67 us  [the longest x1 1.35 us: local(): jnp.concatenate([adapter_down_weight, adapter_up_weight], axis=2)]
    dot_general x3 -> x2, matrix products: 5.59 us -> 4.17 us  [the longest x1 3.9 us: local(): jnp.einsum('rk,kab->rab', picker, adapters_everywhere, preferred_element_...]
  transfers between devices with their start and end apart: 4 -> 4, of which waited for: 2 -> 3; matrix products, arithmetic and copies ran while one was open for 7% -> 6% of each run, Pallas kernels for 0% -> 0%
where the time goes in v1:
time: 187 us; the launch traced here: 186 us
  waiting for transfers between devices  104 us (56%)
  starting transfers between devices  27.5 us (15%)
  blocking collectives  14.7 us (8%)
  between operations  13.7 us (7%)
  local copies, waits for them, and re-layouts  12.1 us (6%)
  matrix products  7.87 us (4%)
  other arithmetic  5.9 us (3%)
    all_gather x1, waiting for transfers between devices, local(): lax.all_gather(adapter_pair, 'req', axis=0, tiled=True)  69.9 us
    all_to_all x1, waiting for transfers between devices, local(): lax.all_to_all(slots, 'tp', split_axis=0, concat_axis=0, tiled=True)  29.2 us
    psum x1, blocking collectives, local(): square_sum = lax.psum(square_part, 'tp')  14.7 us
    all_to_all x1, starting transfers between devices, local(): lax.all_to_all(request_page_table, 'req', split_axis=1, concat_axis=1, ti...  14 us
    all_to_all x1, starting transfers between devices, local(): lax.all_to_all(kv_out, 'req', split_axis=1, concat_axis=1, tiled=True)  6.76 us
    all_to_all x1, starting transfers between devices, local(): lax.all_to_all(slots, 'tp', split_axis=0, concat_axis=0, tiled=True)  6.66 us
    unnamed x33, local copies, waits for them, and re-layouts  5.44 us
    all_to_all x1, waiting for transfers between devices, local(): lax.all_to_all(request_page_table, 'req', split_axis=1, concat_axis=1, ti...  5.04 us
  transfers between devices with their start and end apart: 4, of which 3 were waited for; matrix products, arithmetic and copies ran while one was open for 6% of the time, Pallas kernels for 0%

profile of v1, /device:TPU:6, one launch (start us, length us, event | category | flops | bytes accessed | tf_op | source)
XLA Modules:
  0.0 185.8 jit_solution(3870955451242989684)
XLA Ops:
  6.5 1.4 copy.88
  8.0 14.0 %all-to-all-start = ((s32[2,64,1]{0,2,1:T(1,128)}), s32[2,64,1]{0,2,1:T(1,128)S(1)}, u32[]{:S(2)}, u32[]{:S(2)}) async-start(s32[2,64,1]{0,2,1:T(1,128)} %copy.88), calls=%async_computation | async-start | bytes 65536 | tf_op jit(solution)/shard_map/all_to_all | solution.py:86
  22.0 1.4 pad_maximum_fusion.1
  23.4 1.1 pad_maximum_fusion
  24.5 5.0 %all-to-all-done = s32[2,64,1]{0,2,1:T(1,128)S(1)} async-done(((s32[2,64,1]{0,2,1:T(1,128)}), s32[2,64,1]{0,2,1:T(1,128)S(1)}, u32[]{:S(2)}, u32[]{:S(2)}) %all-to-all-start) | async-done | bytes 544 | tf_op jit(solution)/shard_map/all_to_all | solution.py:86
  29.7 0.7 gather_fusion
  30.4 1.6 copy.90
  32.0 6.8 %all-to-all-start.1 = ((bf16[2,64,16,512]{3,2,0,1:T(8,128)(2,1)}), bf16[2,64,16,512]{3,2,0,1:T(8,128)(2,1)S(1)}, u32[]{:S(2)}, u32[]{:S(2)}) async-start(bf16[2,64,16,512]{3,2,0,1:T(8,128)(2,1)} %copy.90), calls=%async_computation.1 | async-start | bytes 4194304 | tf_op jit(solution)/shard_map/all_to_all | solution.py:90
  38.8 0.7 copy.92
  40.1 0.2 fusion.31
  40.4 0.3 broadcast_and_fusion
  40.8 0.9 fusion.38
  41.7 69.9 %all-gather.2.cloned.1.call-done = bf16[64,16,960]{2,1,0:T(8,128)(2,1)} async-done(((bf16[1,16,960]{2,1,0:T(8,128)(2,1)}), bf16[64,16,960]{2,1,0:T(8,128)(2,1)}) %all-gather.2.cloned.1.call-update) | async-done | bytes 1966096 | tf_op jit(solution)/shard_map/all_gather | solution.py:84
  111.6 3.9 %fusion.10 = bf16[2,16,960]{2,0,1:T(2,128)(2,1)S(1)} fusion(bf16[64,16,960]{2,1,0:T(8,128)(2,1)} %all-gather.2.cloned.1.call-done, s32[2]{0:T(128)S(1)} %fusion.31), kind=kOutput, calls=%fused_computation.19 | convolution fusion | flops 3963008 | bytes 2027528 | tf_op jit(solution)/shard_map/rk,kab->rab/dot_general | solution.py:118
  115.5 0.2 copy.91
  115.7 0.4 copy-done.5
  116.1 1.3 copy-done.1
  117.5 1.4 copy.93
  119.0 0.5 copy-done.2
  119.5 1.5 fusion.37
  121.1 0.7 copy-done.6
  121.9 0.3 fusion.3
  122.3 0.6 convolution_convert_fusion.1
  122.9 1.5 copy-done.3
  124.4 0.7 convolution_convert_fusion
  125.1 0.6 copy.99
  125.9 1.3 maximum_maximum_fusion
  127.1 6.7 %all-to-all-start.2 = ((bf16[8,128,512]{1,2,0:T(8,128)(2,1)}), bf16[8,128,512]{1,2,0:T(8,128)(2,1)S(1)}, u32[]{:S(2)}, u32[]{:S(2)}) async-start(bf16[8,128,512]{1,2,0:T(8,128)(2,1)} %maximum_maximum_fusion), calls=%async_computation.2 | async-start | bytes 2097152 | tf_op jit(solution)/shard_map/all_to_all | solution.py:142
  133.8 29.2 %all-to-all-done.2 = bf16[8,128,512]{1,2,0:T(8,128)(2,1)S(1)} async-done(((bf16[8,128,512]{1,2,0:T(8,128)(2,1)}), bf16[8,128,512]{1,2,0:T(8,128)(2,1)S(1)}, u32[]{:S(2)}, u32[]{:S(2)}) %all-to-all-start.2) | async-done | bytes 1048608 | tf_op jit(solution)/shard_map/all_to_all | solution.py:142
  163.2 0.3 multiply_reduce_fusion
  163.5 14.7 %psum.7 = f32[128]{0:T(128)S(1)} all-reduce(f32[128]{0:T(128)S(1)} %get-tuple-element.12), channel_id=1, replica_groups=mesh['req'=64,'tp'=8] {'tp'}, use_global_device_ids=true, to_apply=%region_10.11 | all-reduce | flops 128 | bytes 1024 | tf_op jit(solution)/shard_map/psum | solution.py:156
  178.2 0.8 add_convert_fusion
  (58 shorter events, 1.8 us)
Async XLA Ops:
  6.5 34.3 %copy-start = (bf16[128,256]{1,0:T(8,128)(2,1)S(1)}, bf16[128,256]{1,0:T(8,128)(2,1)}, u32[]{:S(2)}) copy-start(bf16[128,256]{1,0:T(8,128)(2,1)} %param.17) | copy-start | bytes 196612
  8.0 21.6 %all-to-all-start = ((s32[2,64,1]{0,2,1:T(1,128)}), s32[2,64,1]{0,2,1:T(1,128)S(1)}, u32[]{:S(2)}, u32[]{:S(2)}) async-start(s32[2,64,1]{0,2,1:T(1,128)} %copy.88), calls=%async_computation | async-start | bytes 65536 | tf_op jit(solution)/shard_map/all_to_all | solution.py:86
  22.0 89.6 %all-gather.2.cloned.1.call-start = ((), (), s32[]{:S(2)}) async-start(), calls=%async_computation.3 | async-start | bytes 2129920 | tf_op jit(solution)/shard_map/all_gather | solution.py:84
  32.0 6.8 %copy-start.8 = (bf16[128,256]{1,0:T(8,128)(2,1)S(1)}, bf16[128,256]{1,0:T(8,128)(2,1)}, u32[]{:S(2)}) copy-start(bf16[128,256]{1,0:T(8,128)(2,1)} %param.18) | copy-start | bytes 196612
  32.0 7.5 %copy-start.11 = (s32[2,64]{1,0:T(2,128)S(1)}, s32[2,64]{1,0:T(2,128)}, u32[]{:S(2)}) copy-start(s32[2,64]{1,0:T(2,128)} %param.22) | copy-start | bytes 1540
  32.0 7.8 %copy-start.13 = (s32[1,2]{1,0:T(1,128)S(1)}, s32[1,2]{1,0:T(1,128)}, u32[]{:S(2)}) copy-start(s32[1,2]{1,0:T(1,128)} %param.23) | copy-start | bytes 28
  32.0 8.2 %copy-start.14 = (s32[64]{0:T(128)S(1)}, s32[64]{0:T(128)}, u32[]{:S(2)}) copy-start(s32[64]{0:T(128)} %param.25) | copy-start | bytes 772
  32.0 8.2 %copy-start.15 = (s32[1,2]{1,0:T(1,128)S(1)}, s32[1,2]{1,0:T(1,128)}, u32[]{:S(2)}) copy-start(s32[1,2]{1,0:T(1,128)} %param.24) | copy-start | bytes 28
  32.0 8.8 %copy-start.12 = (bf16[128,512]{1,0:T(8,128)(2,1)S(1)}, bf16[128,512]{1,0:T(8,128)(2,1)}, u32[]{:S(2)}) copy-start(bf16[128,512]{1,0:T(8,128)(2,1)} %param.16) | copy-start | bytes 393220
  32.0 83.5 %all-to-all-start.1 = ((bf16[2,64,16,512]{3,2,0,1:T(8,128)(2,1)}), bf16[2,64,16,512]{3,2,0,1:T(8,128)(2,1)S(1)}, u32[]{:S(2)}, u32[]{:S(2)}) async-start(bf16[2,64,16,512]{3,2,0,1:T(8,128)(2,1)} %copy.90), calls=%async_computation.1 | async-start | bytes 4194304 | tf_op jit(solution)/shard_map/all_to_all | solution.py:90
  115.5 0.6 copy-start.5
  116.1 1.3 copy-start.1
  117.5 2.0 %copy-start.2 = (bf16[2,64,16,512]{3,2,1,0:T(8,128)(2,1)S(1)}, bf16[2,64,16,512]{3,2,1,0:T(8,128)(2,1)}, u32[]{:S(2)}) copy-start(bf16[2,64,16,512]{3,2,1,0:T(8,128)(2,1)} %copy-done.1) | copy-start | bytes 6291460
  121.0 0.9 copy-start.6
  121.1 1.2 copy-start.4
  121.1 1.2 copy-start.9
  122.3 2.0 %copy-start.3 = (bf16[512,3584]{1,0:T(8,128)(2,1)S(1)}, bf16[512,3584]{1,0:T(8,128)(2,1)}, u32[]{:S(2)}) copy-start(bf16[512,3584]{1,0:T(8,128)(2,1)} %param.26) | copy-start | bytes 11010052
  124.4 1.3 slice-start
  127.1 35.8 %all-to-all-start.2 = ((bf16[8,128,512]{1,2,0:T(8,128)(2,1)}), bf16[8,128,512]{1,2,0:T(8,128)(2,1)S(1)}, u32[]{:S(2)}, u32[]{:S(2)}) async-start(bf16[8,128,512]{1,2,0:T(8,128)(2,1)} %maximum_maximum_fusion), calls=%async_computation.2 | async-start | bytes 2097152 | tf_op jit(solution)/shard_map/all_to_all | solution.py:142
  133.8 29.4 %slice-start.1 = ((bf16[2,16,960]{2,0,1:T(2,128)(2,1)}), bf16[2,16,448]{2,0,1:T(2,128)(2,1)S(1)}, s32[]{:S(2)}) async-start(bf16[2,16,960]{2,0,1:T(2,128)(2,1)} %copy-done.5), calls=%async_computation.5 | async-start | bytes 65536 | tf_op jit(solution)/shard_map/slice | solution.py:122
  163.1 15.1 %copy-start.7 = (bf16[128,448]{0,1:T(8,128)(2,1)S(1)}, bf16[128,448]{0,1:T(8,128)(2,1)}, u32[]{:S(2)}) copy-start(bf16[128,448]{0,1:T(8,128)(2,1)} %param.15) | copy-start | bytes 344068
  163.1 15.1 %copy-start.10 = (f32[448]{0:T(512)S(1)}, f32[448]{0:T(512)}, u32[]{:S(2)}) copy-start(f32[448]{0:T(512)} %param.29) | copy-start | bytes 5380
Sparse Core Ops, SparseCore 0:
  26.1 85.3 all-gather.1
